TPU v7x, 512 devices: a whole 4x4x16 slice. The times are simulated.
512 devices in a mesh: tok: 64 (over z, x), head: 8 (over y, core).
Axes of the slice: x: 4, y: 4, z: 16, core: 2. Of those that a mesh axis runs over, the one named last changes fastest.
Arguments:
- tokens: bfloat16 [32768, 2560], P('tok', 'head'), may hold values from -6 to 6
- query_weight: bfloat16 [2560, 2560], P('tok'), may hold values from -0.125 to 0.125
- keyvalue_weight: bfloat16 [2560, 512], P('tok'), may hold values from -0.125 to 0.125
- output_weight: bfloat16 [2560, 2560], P(None, ('head', 'tok')), may hold values from -0.125 to 0.125
- cache: bfloat16 [2048, 2, 128, 256], P(('tok', 'head')), may hold values from -460 to 460
- page_table: int32 [512, 4], P('tok'), may hold values from 0 to 2047, as said below
- parents: int32 [512, 64], P('tok'), may hold values from 0 to 62, as said below
- cache_len: int32 [512], P('tok'), may hold values from 1 to 448, as said below
- accepted_leaf: int32 [512], P('tok'), may hold values from 0 to 63
Outputs:
- attended: bfloat16 [32768, 2560], P('tok', 'head')
- cache_out: bfloat16 [2048, 2, 128, 256], P(('tok', 'head'))
Inputs may be any that keep to these rules, and one draw needn't show every extreme that they name: `page_table`: for every d, row d names each of the pages d * 4 to d * 4 + 3 exactly once, so request d's pages all lie on device d (devices counted tok-major, head-minor). parents[r, 0] = 0, and parents[r, i] < i for i >= 1. `cache_len`: roughly half of the requests hold at most 128 cached positions, the others more than 320.
All inputs are finite; a program needn't handle non-finite values.
Results may differ from a plain program's by a relative error of at most 0.014.
The roundings to bfloat16 on the way count: a program that leaves them out, or rounds other values in their place, can miss the bound.
Values may be sent and summed in bfloat16 or wider, within the bound.
No kernel may reach another device: no remote copies, remote signals or barrier semaphores. Data moves between devices by JAX's collectives and lax.ppermute only.
A program may use at most 64 MiB of HBM per device.

v0:
```python
import math
import jax
import jax.numpy as jnp
from jax import lax
from jax.sharding import PartitionSpec as P

HQ = 10
HD = 256
DRAFT = 64
PAGE = 128
NPR = 4
WINDOW = 256


def ancestry(parent_row):
    node_ids = jnp.arange(DRAFT, dtype=jnp.int32)
    link = (parent_row[:, None] == node_ids[None, :]).astype(jnp.float32)
    reach = jnp.minimum(link + jnp.eye(DRAFT, dtype=jnp.float32), 1.0)
    for sweep in range((DRAFT - 1).bit_length()):
        reach = jnp.minimum(jnp.dot(reach, reach, precision=lax.Precision.HIGHEST), 1.0)
    depth = (jnp.sum(reach, axis=1) - 1.0).astype(jnp.int32)
    return (reach, depth)


def rotate(values, position):
    half = HD // 4
    freq = jnp.exp(jnp.arange(half, dtype=jnp.float32) * (-2.0 * math.log(10000.0) / (HD // 2)))
    angle = position.astype(jnp.float32)[..., None] * freq
    cosine = jnp.cos(angle)
    sine = jnp.sin(angle)
    first = values[..., :half]
    second = values[..., half : 2 * half]
    return jnp.concatenate(
        [first * cosine - second * sine, second * cosine + first * sine, values[..., 2 * half :]],
        axis=-1,
    )


def attend(queries, cache_keys, cache_values, tree_keys, tree_values, lengths, position, reach):
    window_span = cache_keys.shape[1]
    slot_ids = jnp.arange(window_span, dtype=jnp.int32)
    visible = (slot_ids[None, None, :] < lengths[:, None, None]) & (
        slot_ids[None, None, :] > position[:, :, None] - WINDOW
    )
    cache_scores = jnp.einsum(
        "rnhd,rcd->rhnc", queries, cache_keys, preferred_element_type=jnp.float32
    )
    tree_scores = jnp.einsum(
        "rnhd,rmd->rhnm", queries, tree_keys, preferred_element_type=jnp.float32
    )
    cache_scores = jnp.where(visible[:, None], cache_scores, -1e30)
    tree_scores = jnp.where(reach[:, None] > 0.5, tree_scores, -1e30)
    row_peak = jnp.maximum(jnp.max(cache_scores, axis=-1), jnp.max(tree_scores, axis=-1))[..., None]
    cache_weights = jnp.exp(cache_scores - row_peak)
    tree_weights = jnp.exp(tree_scores - row_peak)
    denominator = jnp.sum(cache_weights, axis=-1, keepdims=True) + jnp.sum(
        tree_weights, axis=-1, keepdims=True
    )
    cache_weights = (cache_weights / denominator).astype(jnp.bfloat16)
    tree_weights = (tree_weights / denominator).astype(jnp.bfloat16)
    result = jnp.einsum(
        "rhnc,rcd->rnhd", cache_weights, cache_values, preferred_element_type=jnp.float32
    )
    result = result + jnp.einsum(
        "rhnm,rmd->rnhd", tree_weights, tree_values, preferred_element_type=jnp.float32
    )
    return result.astype(jnp.bfloat16)


def refresh(logical_pages, length, leaf, reach, depth, new_keys, new_values):
    count = logical_pages.shape[0] * logical_pages.shape[2]
    logical = jnp.transpose(logical_pages, (1, 0, 2, 3)).reshape(2, count, HD)
    slot_ids = jnp.arange(count, dtype=jnp.int32)
    on_path = reach[leaf]
    selector = ((on_path[None, :] > 0.5) & (depth[None, :] == slot_ids[:, None] - length)).astype(
        jnp.float32
    )
    placed_keys = jnp.dot(selector, new_keys.astype(jnp.float32), precision=lax.Precision.HIGHEST)
    placed_values = jnp.dot(
        selector, new_values.astype(jnp.float32), precision=lax.Precision.HIGHEST
    )
    placed = jnp.stack([placed_keys, placed_values]).astype(jnp.bfloat16)
    written = jnp.sum(selector, axis=1) > 0.5
    logical = jnp.where(written[None, :, None], placed, logical)
    return jnp.transpose(
        logical.reshape(2, logical_pages.shape[0], logical_pages.shape[2], HD), (1, 0, 2, 3)
    )


def shards(
    tokens,
    query_weight,
    keyvalue_weight,
    output_weight,
    cache,
    page_table,
    parents,
    cache_len,
    accepted_leaf,
):
    head_count = lax.axis_size("head")
    head_index = lax.axis_index("head")
    tok_index = lax.axis_index("tok")
    requests = parents.shape[0]
    assert requests == head_count
    pages_dev = cache.shape[0]
    part_rows = query_weight.shape[0]
    q_cols = HQ * HD // head_count
    kv_cols = 2 * HD // head_count
    out_cols = output_weight.shape[1]
    wq_piece = lax.dynamic_slice_in_dim(query_weight, head_index * q_cols, q_cols, axis=1)
    wkv_piece = lax.dynamic_slice_in_dim(keyvalue_weight, head_index * kv_cols, kv_cols, axis=1)
    flat = jnp.concatenate([wq_piece.reshape(-1), wkv_piece.reshape(-1), output_weight.reshape(-1)])
    stacked = lax.all_gather(flat, "tok", axis=0, tiled=False)
    tok_count = stacked.shape[0]
    n_q = part_rows * q_cols
    n_kv = part_rows * kv_cols
    wq_cols = stacked[:, :n_q].reshape(tok_count * part_rows, q_cols)
    wkv_cols = stacked[:, n_q : n_q + n_kv].reshape(tok_count * part_rows, kv_cols)
    wo_cols = (
        stacked[:, n_q + n_kv :]
        .reshape(tok_count, HQ * HD, out_cols)
        .transpose(1, 0, 2)
        .reshape(HQ * HD, tok_count * out_cols)
    )
    gathered = lax.all_gather(tokens, "head", axis=1, tiled=True)
    wide = gathered.astype(jnp.float32)
    mean_square = jnp.mean(wide * wide, axis=1, keepdims=True)
    normed = (wide * lax.rsqrt(mean_square + 1e-06)).astype(jnp.bfloat16)
    q_part = jnp.dot(normed, wq_cols, preferred_element_type=jnp.float32)
    kv_part = jnp.dot(normed, wkv_cols, preferred_element_type=jnp.float32)
    both = jnp.concatenate([q_part, kv_part], axis=1)
    mine = lax.all_to_all(both, "head", 0, 1, tiled=True)
    mine = mine.reshape(DRAFT, head_count, q_cols + kv_cols)
    q_pre = mine[:, :, :q_cols].reshape(DRAFT, HQ, HD)
    kv_pre = mine[:, :, q_cols:].reshape(DRAFT, 2 * HD)
    parent_row = lax.dynamic_index_in_dim(parents, head_index, 0, keepdims=False)
    length = lax.dynamic_index_in_dim(cache_len, head_index, 0, keepdims=False)
    leaf = lax.dynamic_index_in_dim(accepted_leaf, head_index, 0, keepdims=False)
    reach, depth = ancestry(parent_row)
    position = length + depth
    queries = (rotate(q_pre, position[:, None]) * HD ** (-0.5)).astype(jnp.bfloat16)
    tree_keys = rotate(kv_pre[:, :HD], position).astype(jnp.bfloat16)
    tree_values = kv_pre[:, HD:].astype(jnp.bfloat16)
    device = tok_index * head_count + head_index
    own_table = (
        lax.dynamic_index_in_dim(page_table, head_index, 0, keepdims=False) - device * pages_dev
    )
    own_pages = jnp.take(cache, own_table, axis=0)
    cache_keys = own_pages[:, 0].reshape(NPR * PAGE, HD)
    cache_values = own_pages[:, 1].reshape(NPR * PAGE, HD)
    result = attend(
        queries[None],
        cache_keys[None],
        cache_values[None],
        tree_keys[None],
        tree_values[None],
        length[None],
        position[None],
        reach[None],
    )
    mixed = lax.all_gather(result.reshape(DRAFT, HQ * HD), "head", axis=0, tiled=True)
    summed = jnp.zeros((mixed.shape[0], wo_cols.shape[1]), jnp.float32)
    for group in range(head_count):
        head_ids = [k for k in range(group, HQ, head_count)]
        if not head_ids:
            continue
        columns = jnp.concatenate([mixed[:, k * HD : (k + 1) * HD] for k in head_ids], axis=1)
        rows = jnp.concatenate([wo_cols[k * HD : (k + 1) * HD] for k in head_ids], axis=0)
        partial_value = jnp.dot(columns, rows, preferred_element_type=jnp.float32)
        summed = summed + partial_value.astype(jnp.bfloat16).astype(jnp.float32)
    attended = summed.astype(jnp.bfloat16)
    new_pages = refresh(own_pages, length, leaf, reach, depth, tree_keys, tree_values)
    matches = (own_table[:, None] == jnp.arange(pages_dev, dtype=jnp.int32)[None, :]).astype(
        jnp.int32
    )
    inverse = jnp.sum(matches * jnp.arange(pages_dev, dtype=jnp.int32)[:, None], axis=0)
    cache_out = jnp.take(new_pages, inverse, axis=0)
    return (attended, cache_out)


def solution(mesh):
    in_specs = (
        P("tok", "head"),
        P("tok", None),
        P("tok", None),
        P(None, ("head", "tok")),
        P(("tok", "head"), None, None, None),
        P("tok", None),
        P("tok", None),
        P("tok"),
        P("tok"),
    )
    out_specs = (P("tok", "head"), P(("tok", "head"), None, None, None))
    return jax.shard_map(shards, mesh=mesh, in_specs=in_specs, out_specs=out_specs, check_vma=False)
```

profile of v0, /device:TPU:1, one launch (start us, length us, event | category | flops | bytes accessed | tf_op | source)
XLA Modules:
  0.0 285.6 jit_solution(11939136876773440064)
XLA Ops:
  7.2 0.7 all-gather.6.cloned.1.call-update
  8.0 0.9 constant_dynamic-slice_fusion.2
  9.0 0.8 constant_dynamic-slice_fusion.1
  9.8 1.2 copy.62
  11.0 1.0 reshape.334
  12.0 0.7 reshape.362
  12.7 1.3 dynamic_slice.29
  15.4 1.2 dynamic_slice.25
  16.7 0.7 fusion.70
  19.5 0.7 iota_subtract_fusion
  20.4 29.1 %all-gather.6.cloned.1.call-done = bf16[512,2560]{0,1:T(8,128)(2,1)} async-done(((bf16[512,320]{0,1:T(8,128)(2,1)}), bf16[512,2560]{0,1:T(8,128)(2,1)}) %all-gather.6.cloned.1.call-update) | async-done | bytes 2621456 | tf_op jit(solution)/shard_map/all_gather | solution.py:126
  49.5 2.4 fusion
  51.9 146.4 %all-gather.10.cloned.1.call-done = bf16[64,1,28160]{2,1,0:T(2,128)(2,1)} async-done(((bf16[1,1,28160]{2,1,0:T(2,128)(2,1)}), bf16[64,1,28160]{2,1,0:T(2,128)(2,1)}) %all-gather.10.cloned.1.call-update) | async-done | bytes 3604496 | tf_op jit(solution)/shard_map/all_gather | solution.py:114
  198.3 3.5 %copy.97 = bf16[64,1,28160]{2,0,1:T(8,128)(2,1)S(1)} copy(bf16[64,1,28160]{2,1,0:T(2,128)(2,1)} %all-gather.10.cloned.1.call-done) | data formatting | bytes 7208960
  201.7 1.4 fusion.79
  203.1 2.5 reshape.335
  206.0 3.6 %fusion.4 = f32[512,320]{0,1:T(8,128)S(1)} fusion(bf16[2560,320]{1,0:T(8,128)(2,1)} %reshape.335, bf16[512,2560]{0,1:T(8,128)(2,1)} %all-gather.6.cloned.1.call-done, f32[512]{0:T(512)S(1)} %add_rsqrt_fusion), kind=kOutput, calls=%fused_computation.8 | convolution fusion | flops 842792960 | bytes 4917248 | tf_op jit(solution)/shard_map/dot_general | solution.py:130
  209.7 0.7 fusion.2
  210.5 1.2 copy.63
  211.6 12.7 %all-to-all-start = ((f32[8,64,384]{2,1,0:T(8,128)}), f32[8,64,384]{2,1,0:T(8,128)S(1)}, u32[]{:S(2)}, u32[]{:S(2)}) async-start(f32[8,64,384]{2,1,0:T(8,128)} %bitcast.6), calls=%async_computation | async-start | bytes 1572864 | tf_op jit(solution)/shard_map/all_to_all | solution.py:133
  224.3 0.6 iota_compare_fusion.6
  225.1 0.6 gather_fusion
  225.7 0.7 add_add_fusion
  226.4 10.0 %all-to-all-done = f32[8,64,384]{2,1,0:T(8,128)S(1)} async-done(((f32[8,64,384]{2,1,0:T(8,128)}), f32[8,64,384]{2,1,0:T(8,128)S(1)}, u32[]{:S(2)}, u32[]{:S(2)}) %all-to-all-start) | async-done | bytes 786464 | tf_op jit(solution)/shard_map/all_to_all | solution.py:133
  237.3 0.5 copy.64
  237.7 0.4 reshape.337
  239.0 1.0 fusion.36
  240.7 0.5 fusion.83
  242.5 0.7 copy.90
  243.5 2.9 %copy.72 = bf16[64,12800]{0,1:T(8,128)(2,1)} copy(bf16[64,12800]{1,0:T(8,128)(2,1)S(1)} %copy-done.1) | data formatting | bytes 3276800 | tf_op jit(solution)/shard_map/slice | solution.py:121
  246.4 7.1 %reshape.342 = bf16[64,2560,5]{0,2,1:T(8,128)(2,1)} reshape(bf16[64,12800]{0,1:T(8,128)(2,1)} %copy.72) | data formatting | bytes 3276800 | tf_op jit(solution)/shard_map/reshape | solution.py:122
  253.5 4.9 %fusion.78 = (bf16[256,64,5]{1,2,0:T(8,128)(2,1)S(1)}, bf16[256,64,5]{1,2,0:T(8,128)(2,1)S(1)}, bf16[256,64,5]{1,2,0:T(8,128)(2,1)S(1)}, bf16[256,64,5]{1,2,0:T(...) fusion(bf16[2560,64,5]{1,2,0:T(8,128)(2,1)} %bitcast.112), kind=kLoop, calls=%fused_computation.143 | loop fusion | bytes 3276800 | tf_op jit(solution)/shard_map/slice | solution.py:169
  258.4 1.5 copy.73
  259.9 0.7 slice.155
  260.7 1.5 copy.74
  262.1 0.7 slice.157
  262.9 1.5 copy.75
  264.4 0.7 slice.161
  265.1 1.5 copy.76
  266.6 0.7 slice.163
  267.4 1.5 copy.77
  268.9 0.7 slice.166
  269.6 0.4 copy.78
  270.0 0.7 slice.169
  272.9 0.6 gather_fusion.1
  273.5 0.9 broadcast_select_fusion
  274.4 1.4 fusion.80
  278.1 1.0 fusion.10
  (93 shorter events, 10.5 us)
Async XLA Ops:
  7.2 217.9 %copy-start = (bf16[4,2,128,256]{3,2,1,0:T(8,128)(2,1)S(1)}, bf16[4,2,128,256]{3,2,1,0:T(8,128)(2,1)}, u32[]{:S(2)}) copy-start(bf16[4,2,128,256]{3,2,1,0:T(8,128)(2,1)} %param.15) | copy-start | bytes 1572868
  7.2 12.1 %copy-start.11 = (s32[8,4]{0,1:T(4,128)S(1)}, s32[8,4]{0,1:T(4,128)}, u32[]{:S(2)}) copy-start(s32[8,4]{0,1:T(4,128)} %param.16) | copy-start | bytes 388
  7.2 42.3 %all-gather.6.cloned.1.call-start = ((), (), s32[]{:S(2)}) async-start(), calls=%async_computation.1 | async-start | bytes 2949120 | tf_op jit(solution)/shard_map/all_gather | solution.py:126
  7.9 190.3 %all-gather.10.cloned.1.call-start = ((), (), s32[]{:S(2)}) async-start(), calls=%async_computation.3 | async-start | bytes 7321600 | tf_op jit(solution)/shard_map/all_gather | solution.py:114
  206.0 3.7 %copy-start.2 = (bf16[512,2560]{0,1:T(8,128)(2,1)S(1)}, bf16[512,2560]{0,1:T(8,128)(2,1)}, u32[]{:S(2)}) copy-start(bf16[512,2560]{0,1:T(8,128)(2,1)} %all-gather.6.cloned.1.call-done) | copy-start | bytes 7864324
  211.6 24.9 %all-to-all-start = ((f32[8,64,384]{2,1,0:T(8,128)}), f32[8,64,384]{2,1,0:T(8,128)S(1)}, u32[]{:S(2)}, u32[]{:S(2)}) async-start(f32[8,64,384]{2,1,0:T(8,128)} %bitcast.6), calls=%async_computation | async-start | bytes 1572864 | tf_op jit(solution)/shard_map/all_to_all | solution.py:133
  224.3 50.1 %all-gather.8.cloned.1.call-start = ((), (), s32[]{:S(2)}) async-start(), calls=%async_computation.2 | async-start | bytes 2949120 | tf_op jit(solution)/shard_map/all_gather | solution.py:162
  242.0 1.5 copy-start.1
  270.0 2.9 %copy-start.4 = (bf16[4,2,128,256]{3,2,1,0:T(8,128)(2,1)S(1)}, bf16[4,2,128,256]{3,2,1,0:T(8,128)(2,1)}, u32[]{:S(2)}) copy-start(bf16[4,2,128,256]{3,2,1,0:T(8,128)(2,1)} %get-tuple-element.3) | copy-start | bytes 1572868
  272.3 3.5 %copy-start.9 = (bf16[256,320]{0,1:T(8,128)(2,1)S(1)}, bf16[256,320]{0,1:T(8,128)(2,1)}, u32[]{:S(2)}) copy-start(bf16[256,320]{0,1:T(8,128)(2,1)} %slice.155) | copy-start | bytes 491524
  272.4 3.5 %copy-start.10 = (bf16[256,320]{0,1:T(8,128)(2,1)S(1)}, bf16[256,320]{0,1:T(8,128)(2,1)}, u32[]{:S(2)}) copy-start(bf16[256,320]{0,1:T(8,128)(2,1)} %slice.157) | copy-start | bytes 491524
  273.5 2.8 copy-start.5
  273.5 2.8 copy-start.6
  274.4 2.2 copy-start.7
  274.4 2.2 copy-start.3
  275.9 1.1 copy-start.8
Sparse Core Ops, SparseCore 0:
  10.1 39.3 all-gather.5
  53.1 145.1 all-gather.9
  243.4 27.9 all-gather.7
where the time goes:
time: 287 us; the launch traced here: 286 us
  waiting for transfers between devices  186 us (65%)
  local copies, waits for them, and re-layouts  51.5 us (18%)
  between operations  16.5 us (6%)
  starting transfers between devices  12.8 us (4%)
  matrix products  10.8 us (4%)
  other arithmetic  7.81 us (3%)
    all_gather x1, waiting for transfers between devices, shards(): stacked = lax.all_gather(flat, 'tok', axis=0, tiled=False)  146 us
    all_gather x1, waiting for transfers between devices, shards(): gathered = lax.all_gather(tokens, 'head', axis=1, tiled=True)  29.1 us
    slice x21, local copies, waits for them, and re-layouts, shards(): wo_cols[k * HD:(k + 1) * HD]  19.2 us
    all_to_all x1, starting transfers between devices, shards(): mine = lax.all_to_all(both, 'head', 0, 1, tiled=True)  12.7 us
    all_to_all x1, waiting for transfers between devices, shards(): mine = lax.all_to_all(both, 'head', 0, 1, tiled=True)  10 us
    reshape x1, local copies, waits for them, and re-layouts, shards(): wo_cols = stacked[:, n_q + n_kv:].reshape(tok_count, HQ * HD, out_cols).t...  7.08 us
    unnamed x29, local copies, waits for them, and re-layouts  6.45 us
  transfers between devices with their start and end apart: 4, of which 3 were waited for; matrix products, arithmetic and copies ran while one was open for 16% of the time, Pallas kernels for 0%

commit v1 on v0

--- a/solution.py
+++ b/solution.py
@@ -123,7 +123,10 @@
         .transpose(1, 0, 2)
         .reshape(HQ * HD, tok_count * out_cols)
     )
-    gathered = lax.all_gather(tokens, "head", axis=1, tiled=True)
+    taken_in = lax.all_to_all(
+        jnp.stack([tokens for _ in range(lax.axis_size("head"))]), "head", 0, 0
+    )
+    gathered = jnp.concatenate(taken_in, axis=1)
     wide = gathered.astype(jnp.float32)
     mean_square = jnp.mean(wide * wide, axis=1, keepdims=True)
     normed = (wide * lax.rsqrt(mean_square + 1e-06)).astype(jnp.bfloat16)

time: 287 us -> 251 us (0.87)
  waiting for transfers between devices: 186 us -> 139 us
  starting transfers between devices: 12.8 us -> 23.2 us
    all_gather x1, waiting for transfers between devices: 146 us -> 103 us  [shards(): stacked = lax.all_gather(flat, 'tok', axis=0, tiled=False)]
    all_gather x1 -> x0, waiting for transfers between devices: 29.1 us -> none  [shards(): gathered = lax.all_gather(tokens, 'head', axis=1, tiled=True)]
    all_to_all x0 -> x1, waiting for transfers between devices: none -> 25.3 us  [shards(): lax.all_to_all(jnp.stack([tokens for _ in range(lax.axis_size('head'))]),...]
    all_to_all x0 -> x1, starting transfers between devices: none -> 10.5 us  [shards(): lax.all_to_all(jnp.stack([tokens for _ in range(lax.axis_size('head'))]),...]
    unnamed x29 -> x33, local copies, waits for them, and re-layouts: 6.45 us -> 6.52 us
where the time goes in v1:
time: 251 us; the launch traced here: 250 us
  waiting for transfers between devices  139 us (55%)
  local copies, waits for them, and re-layouts  53.7 us (21%)
  starting transfers between devices  23.2 us (9%)
  between operations  16.4 us (7%)
  matrix products  9.74 us (4%)
  other arithmetic  8.17 us (3%)
    all_gather x1, waiting for transfers between devices, shards(): stacked = lax.all_gather(flat, 'tok', axis=0, tiled=False)  103 us
    all_to_all x1, waiting for transfers between devices, shards(): lax.all_to_all(jnp.stack([tokens for _ in range(lax.axis_size('head'))]),...  25.3 us
    slice x21, local copies, waits for them, and re-layouts, shards(): wo_cols[k * HD:(k + 1) * HD]  16.9 us
    all_to_all x1, starting transfers between devices, shards(): mine = lax.all_to_all(both, 'head', 0, 1, tiled=True)  12.7 us
    all_to_all x1, waiting for transfers between devices, shards(): mine = lax.all_to_all(both, 'head', 0, 1, tiled=True)  10.7 us
    all_to_all x1, starting transfers between devices, shards(): lax.all_to_all(jnp.stack([tokens for _ in range(lax.axis_size('head'))]),...  10.5 us
    reshape x1, local copies, waits for them, and re-layouts, shards(): wo_cols = stacked[:, n_q + n_kv:].reshape(tok_count, HQ * HD, out_cols).t...  7.08 us
    unnamed x33, local copies, waits for them, and re-layouts  6.52 us
  transfers between devices with their start and end apart: 4, of which 3 were waited for; matrix products, arithmetic and copies ran while one was open for 16% of the time, Pallas kernels for 0%

profile of v1, /device:TPU:1, one launch (start us, length us, event | category | flops | bytes accessed | tf_op | source)
XLA Modules:
  0.0 249.8 jit_solution(5478837662127926145)
XLA Ops:
  7.2 0.8 constant_dynamic-slice_fusion.1
  8.1 0.9 constant_dynamic-slice_fusion.2
  9.1 1.2 copy.63
  10.3 1.0 reshape.350
  11.3 0.7 reshape.378
  12.0 2.8 %stack.8 = bf16[8,512,320]{1,2,0:T(8,128)(2,1)} broadcast(bf16[512,320]{0,1:T(8,128)(2,1)} %param.11), dimensions={1,2} | broadcast | bytes 2949120 | tf_op jit(solution)/shard_map/stack | solution.py:127
  14.8 10.5 %all-to-all-start = ((bf16[8,512,320]{1,2,0:T(8,128)(2,1)}), bf16[8,512,320]{1,2,0:T(8,128)(2,1)S(1)}, u32[]{:S(2)}, u32[]{:S(2)}) async-start(bf16[8,512,320]{1,2,0:T(8,128)(2,1)} %stack.8), calls=%async_computation | async-start | bytes 5242880 | tf_op jit(solution)/shard_map/all_to_all | solution.py:126
  25.3 0.7 fusion.66
  26.4 0.6 dynamic_slice.29
  28.1 0.6 dynamic_slice.25
  30.3 0.7 iota_compare_fusion.6
  31.0 0.7 iota_subtract_fusion
  31.8 25.3 %all-to-all-done = bf16[8,512,320]{1,2,0:T(8,128)(2,1)S(1)} async-done(((bf16[8,512,320]{1,2,0:T(8,128)(2,1)}), bf16[8,512,320]{1,2,0:T(8,128)(2,1)S(1)}, u32[]{:S(2)}, u32[]{:S(2)}) %all-to-all-start) | async-done | bytes 2621472 | tf_op jit(solution)/shard_map/all_to_all | solution.py:126
  57.1 0.6 fusion
  57.8 2.1 fusion.1
  59.8 102.5 %all-gather.7.cloned.1.call-done = bf16[64,1,28160]{2,1,0:T(2,128)(2,1)} async-done(((bf16[1,1,28160]{2,1,0:T(2,128)(2,1)}), bf16[64,1,28160]{2,1,0:T(2,128)(2,1)}) %all-gather.7.cloned.1.call-update) | async-done | bytes 3604496 | tf_op jit(solution)/shard_map/all_gather | solution.py:114
  162.4 3.5 %copy.98 = bf16[64,1,28160]{2,0,1:T(8,128)(2,1)S(1)} copy(bf16[64,1,28160]{2,1,0:T(2,128)(2,1)} %all-gather.7.cloned.1.call-done) | data formatting | bytes 7208960
  165.9 1.9 fusion.75
  167.8 1.2 reshape.352
  169.0 4.1 %reshape.351 = bf16[2560,320]{1,0:T(8,128)(2,1)} reshape(bf16[64,12800]{1,0:T(8,128)(2,1)} %get-tuple-element.16) | data formatting | bytes 3276800 | tf_op jit(solution)/shard_map/reshape | solution.py:118
  173.2 2.7 %fusion.84 = f32[512,320]{0,1:T(8,128)S(1)} fusion(bf16[512,2560]{0,1:T(8,128)(2,1)S(1)} %bitcast.120, bf16[2560,320]{1,0:T(8,128)(2,1)} %reshape.351), kind=kOutput, calls=%fused_computation.149 | convolution fusion | flops 838860800 | bytes 4915200 | tf_op jit(solution)/shard_map/dot_general | solution.py:133
  175.9 0.6 fusion.85
  176.5 1.1 copy.64
  177.7 12.7 %all-to-all-start.1 = ((f32[8,64,384]{2,1,0:T(8,128)}), f32[8,64,384]{2,1,0:T(8,128)S(1)}, u32[]{:S(2)}, u32[]{:S(2)}) async-start(f32[8,64,384]{2,1,0:T(8,128)} %bitcast.9), calls=%async_computation.1 | async-start | bytes 1572864 | tf_op jit(solution)/shard_map/all_to_all | solution.py:136
  190.5 0.6 gather_fusion
  191.1 0.7 add_add_fusion
  191.9 10.7 %all-to-all-done.1 = f32[8,64,384]{2,1,0:T(8,128)S(1)} async-done(((f32[8,64,384]{2,1,0:T(8,128)}), f32[8,64,384]{2,1,0:T(8,128)S(1)}, u32[]{:S(2)}, u32[]{:S(2)}) %all-to-all-start.1) | async-done | bytes 786464 | tf_op jit(solution)/shard_map/all_to_all | solution.py:136
  203.3 0.5 copy.65
  205.0 1.0 fusion.32
  206.8 0.5 fusion.79
  208.5 0.7 copy.91
  209.6 2.9 %copy.73 = bf16[64,12800]{0,1:T(8,128)(2,1)} copy(bf16[64,12800]{1,0:T(8,128)(2,1)S(1)} %copy-done.3) | data formatting | bytes 3276800 | tf_op jit(solution)/shard_map/slice | solution.py:121
  212.5 7.1 %reshape.358 = bf16[64,2560,5]{0,2,1:T(8,128)(2,1)} reshape(bf16[64,12800]{0,1:T(8,128)(2,1)} %copy.73) | data formatting | bytes 3276800 | tf_op jit(solution)/shard_map/reshape | solution.py:122
  219.6 5.0 %fusion.74 = (bf16[256,64,5]{1,2,0:T(8,128)(2,1)}, bf16[256,64,5]{1,2,0:T(8,128)(2,1)}, bf16[256,64,5]{1,2,0:T(8,128)(2,1)}, bf16[256,64,5]{1,2,0:T(8,128)(2,1)}...) fusion(bf16[2560,64,5]{1,2,0:T(8,128)(2,1)} %bitcast.117), kind=kLoop, calls=%fused_computation.141 | loop fusion | bytes 3276800 | tf_op jit(solution)/shard_map/slice | solution.py:172
  224.5 1.5 copy.83
  226.0 0.7 slice.181
  226.8 1.5 copy.82
  228.2 0.7 slice.178
  229.0 1.5 copy.81
  230.5 0.7 slice.175
  231.2 1.5 copy.80
  232.7 0.7 slice.172
  235.6 0.4 copy.75
  236.1 0.4 copy.74
  236.7 0.6 gather_fusion.1
  237.3 0.9 broadcast_select_fusion
  238.2 1.4 fusion.76
  241.9 1.0 fusion.6
  (98 shorter events, 10.8 us)
Async XLA Ops:
  7.2 183.3 %copy-start = (bf16[4,2,128,256]{3,2,1,0:T(8,128)(2,1)S(1)}, bf16[4,2,128,256]{3,2,1,0:T(8,128)(2,1)}, u32[]{:S(2)}) copy-start(bf16[4,2,128,256]{3,2,1,0:T(8,128)(2,1)} %param.15) | copy-start | bytes 1572868
  7.2 155.2 %all-gather.7.cloned.1.call-start = ((), (), s32[]{:S(2)}) async-start(), calls=%async_computation.3 | async-start | bytes 7321600 | tf_op jit(solution)/shard_map/all_gather | solution.py:114
  14.8 11.6 %copy-start.12 = (s32[8]{0:T(128)S(1)}, s32[8]{0:T(128)}, u32[]{:S(2)}) copy-start(s32[8]{0:T(128)} %param.19) | copy-start | bytes 100
  14.8 13.4 %copy-start.13 = (s32[8]{0:T(128)S(1)}, s32[8]{0:T(128)}, u32[]{:S(2)}) copy-start(s32[8]{0:T(128)} %param.18) | copy-start | bytes 100
  14.8 15.3 %copy-start.11 = (s32[8,4]{0,1:T(4,128)S(1)}, s32[8,4]{0,1:T(4,128)}, u32[]{:S(2)}) copy-start(s32[8,4]{0,1:T(4,128)} %param.16) | copy-start | bytes 388
  14.8 42.3 %all-to-all-start = ((bf16[8,512,320]{1,2,0:T(8,128)(2,1)}), bf16[8,512,320]{1,2,0:T(8,128)(2,1)S(1)}, u32[]{:S(2)}, u32[]{:S(2)}) async-start(bf16[8,512,320]{1,2,0:T(8,128)(2,1)} %stack.8), calls=%async_computation | async-start | bytes 5242880 | tf_op jit(solution)/shard_map/all_to_all | solution.py:126
  167.8 5.4 %copy-start.2 = (bf16[8,512,320]{1,2,0:T(8,128)(2,1)S(1)}, bf16[8,512,320]{1,2,0:T(8,128)(2,1)}, u32[]{:S(2)}) copy-start(bf16[8,512,320]{1,2,0:T(8,128)(2,1)} %fusion.1) | copy-start | bytes 7864324
  173.2 2.7 %copy-start.5 = (bf16[2560,64]{1,0:T(8,128)(2,1)S(1)}, bf16[2560,64]{1,0:T(8,128)(2,1)}, u32[]{:S(2)}) copy-start(bf16[2560,64]{1,0:T(8,128)(2,1)} %reshape.352) | copy-start | bytes 983044
  177.7 24.9 %all-to-all-start.1 = ((f32[8,64,384]{2,1,0:T(8,128)}), f32[8,64,384]{2,1,0:T(8,128)S(1)}, u32[]{:S(2)}, u32[]{:S(2)}) async-start(f32[8,64,384]{2,1,0:T(8,128)} %bitcast.9), calls=%async_computation.1 | async-start | bytes 1572864 | tf_op jit(solution)/shard_map/all_to_all | solution.py:136
  190.4 47.8 %all-gather.5.cloned.1.call-start = ((), (), s32[]{:S(2)}) async-start(), calls=%async_computation.2 | async-start | bytes 2949120 | tf_op jit(solution)/shard_map/all_gather | solution.py:165
  208.1 1.5 copy-start.3
  234.4 2.2 copy-start.6
  238.2 2.2 copy-start.4
  240.0 1.0 copy-start.10
  240.3 0.9 copy-start.9
  240.6 0.9 copy-start.8
  240.9 1.0 copy-start.7
  241.0 2.0 copy-start.1
Sparse Core Ops, SparseCore 0:
  12.1 150.2 all-gather.6
  209.4 27.9 all-gather.4
